TPU v7x, 256 devices: a whole 4x4x8 slice. The times are simulated.
256 devices in a mesh: wide: 32 (over y, x, core), narrow: 8 (over z).
Axes of the slice: x: 4, y: 4, z: 8, core: 2. Of those that a mesh axis runs over, the one named last changes fastest.
Arguments:
- up_grads: float32 [32, 192, 11008], P('wide', 'narrow'), may hold values from -6 to 6, as said below
- down_grads: float32 [32, 512, 4096], P('wide', 'narrow'), may hold values from -6 to 6, as said below
- gain_grads: float32 [32, 4096], P('wide', 'narrow'), may hold values from -6 to 6
- up_master: float32 [192, 11008], P('narrow', 'wide'), may hold values from -60 to 60, as said below
- down_master: float32 [512, 4096], P('narrow', 'wide'), may hold values from -60 to 60, as said below
- gain_master: float32 [4096], P(('narrow', 'wide')), may hold values from 0.5 to 1.5
- up_first: float32 [192, 11008], P('narrow', 'wide'), may hold values from -1.8 to 1.8, as said below
- down_first: float32 [512, 4096], P('narrow', 'wide'), may hold values from -1.8 to 1.8, as said below
- gain_first: float32 [4096], P(('narrow', 'wide')), may hold values from -4 to 4
- up_second: float32 [192, 11008], P('narrow', 'wide'), may hold values from 0.01 to 1
- down_second: float32 [512, 4096], P('narrow', 'wide'), may hold values from 0.01 to 1
- gain_second: float32 [4096], P(('narrow', 'wide')), may hold values from 0.01 to 1
Outputs:
- up_first_new: float32 [192, 11008], P('narrow', 'wide')
- up_second_new: float32 [192, 11008], P('narrow', 'wide')
- up_master_new: float32 [192, 11008], P('narrow', 'wide')
- up_weights: bfloat16 [192, 11008], replicated
- down_first_new: float32 [512, 4096], P('narrow', 'wide')
- down_second_new: float32 [512, 4096], P('narrow', 'wide')
- down_master_new: float32 [512, 4096], P('narrow', 'wide')
- down_weights: bfloat16 [512, 4096], replicated
- gain_first_new: float32 [4096], P(('narrow', 'wide'))
- gain_second_new: float32 [4096], P(('narrow', 'wide'))
- gain_master_new: float32 [4096], P(('narrow', 'wide'))
- gain_weights: bfloat16 [4096], replicated
Inputs may be any that keep to these rules, and one draw needn't show every extreme that they name: `up_master`: finite real entries. `down_master`: finite real entries. `up_grads`: finite real entries. `down_grads`: finite real entries. `up_first`: finite real entries. `down_first`: finite real entries.
All inputs are finite; a program needn't handle non-finite values.
Results may differ from a plain program's by a relative error of at most 0.001.
Values may be sent and summed in bfloat16 or wider, within the bound.
No kernel may reach another device: no remote copies, remote signals or barrier semaphores. Data moves between devices by JAX's collectives and lax.ppermute only.
A program may use at most 64 MiB of HBM per device.

v0:
```python
import jax
import jax.numpy as jnp
from jax import lax
from jax.sharding import PartitionSpec as P

BETA_ONE = 0.9
BETA_TWO = 0.999
EPSILON = 1e-06
LEARN_RATE = 0.05
DECAY_RATE = 0.01
CORRECT_FIRST = 1.0 - 0.9**10
CORRECT_SECOND = 1.0 - 0.999**10
LANES = 128


def moments(grad_sum, master, first, second, decay):
    first_new = BETA_ONE * first + (1.0 - BETA_ONE) * grad_sum
    second_new = BETA_TWO * second + (1.0 - BETA_TWO) * grad_sum * grad_sum
    update = (
        first_new / CORRECT_FIRST / (jnp.sqrt(second_new / CORRECT_SECOND) + EPSILON)
        + decay * master
    )
    return (first_new, second_new, update)


def finish(master, update, weight_sq, update_sq):
    trust = jnp.sqrt(weight_sq) / (jnp.sqrt(update_sq) + EPSILON)
    return master - LEARN_RATE * trust * update


def padded(total):
    return -(-total // LANES) * LANES


def body(
    up_grads,
    down_grads,
    gain_grads,
    up_master,
    down_master,
    gain_master,
    up_first,
    down_first,
    gain_first,
    up_second,
    down_second,
    gain_second,
):
    n_wide = lax.axis_size("wide")
    n_narrow = lax.axis_size("narrow")
    up_rows, up_cols = up_master.shape
    down_rows, down_cols = down_master.shape
    gain_cols = gain_master.shape[0]
    up_size = up_rows * up_cols
    down_size = down_rows * down_cols
    total = up_size + down_size + gain_cols
    width = padded(total)
    weight_sums = (
        jnp.sum(up_master * up_master),
        jnp.sum(down_master * down_master),
        jnp.sum(gain_master * gain_master),
    )
    up_part = up_grads[0].reshape(up_rows, n_wide, up_cols).transpose(1, 0, 2)
    down_part = down_grads[0].reshape(down_rows, n_wide, down_cols).transpose(1, 0, 2)
    gain_part = gain_grads.reshape(n_wide, gain_cols)
    packed = jnp.concatenate(
        [
            up_part.reshape(n_wide, up_size),
            down_part.reshape(n_wide, down_size),
            gain_part,
            jnp.zeros((n_wide, width - total), jnp.float32),
        ],
        axis=1,
    ).reshape(n_wide, width // LANES, LANES)
    summed = lax.psum_scatter(packed, "wide", scatter_dimension=0, tiled=True)
    summed = summed.reshape(width)
    up_sum = summed[:up_size].reshape(up_rows, up_cols)
    down_sum = summed[up_size : up_size + down_size].reshape(down_rows, down_cols)
    gain_sum = summed[up_size + down_size : total]
    up_first_new, up_second_new, up_update = moments(
        up_sum, up_master, up_first, up_second, DECAY_RATE
    )
    down_first_new, down_second_new, down_update = moments(
        down_sum, down_master, down_first, down_second, DECAY_RATE
    )
    gain_first_new, gain_second_new, gain_update = moments(
        gain_sum, gain_master, gain_first, gain_second, 0.0
    )
    weight_sums, update_sums = lax.psum(
        (
            weight_sums,
            (
                jnp.sum(up_update * up_update),
                jnp.sum(down_update * down_update),
                jnp.sum(gain_update * gain_update),
            ),
        ),
        ("wide", "narrow"),
    )
    up_master_new = finish(up_master, up_update, weight_sums[0], update_sums[0])
    down_master_new = finish(down_master, down_update, weight_sums[1], update_sums[1])
    gain_master_new = finish(gain_master, gain_update, weight_sums[2], update_sums[2])
    low = jnp.concatenate(
        [
            up_master_new.astype(jnp.bfloat16).reshape(up_size),
            down_master_new.astype(jnp.bfloat16).reshape(down_size),
            gain_master_new.astype(jnp.bfloat16),
            jnp.zeros((width - total,), jnp.bfloat16),
        ]
    ).reshape(1, width // LANES, LANES)
    whole = lax.all_gather(low, ("narrow", "wide"), axis=0, tiled=True)
    whole = whole.reshape(n_narrow, n_wide, width)
    up_weights = (
        whole[:, :, :up_size]
        .reshape(n_narrow, n_wide, up_rows, up_cols)
        .transpose(0, 2, 1, 3)
        .reshape(n_narrow * up_rows, n_wide * up_cols)
    )
    down_weights = (
        whole[:, :, up_size : up_size + down_size]
        .reshape(n_narrow, n_wide, down_rows, down_cols)
        .transpose(0, 2, 1, 3)
        .reshape(n_narrow * down_rows, n_wide * down_cols)
    )
    gain_weights = whole[:, :, up_size + down_size : total].reshape(-1)
    return (
        up_first_new,
        up_second_new,
        up_master_new,
        up_weights,
        down_first_new,
        down_second_new,
        down_master_new,
        down_weights,
        gain_first_new,
        gain_second_new,
        gain_master_new,
        gain_weights,
    )


def solution(mesh):
    return jax.shard_map(
        body,
        mesh=mesh,
        in_specs=(
            P("wide", "narrow", None),
            P("wide", "narrow", None),
            P("wide", "narrow"),
            P("narrow", "wide"),
            P("narrow", "wide"),
            P(("narrow", "wide")),
            P("narrow", "wide"),
            P("narrow", "wide"),
            P(("narrow", "wide")),
            P("narrow", "wide"),
            P("narrow", "wide"),
            P(("narrow", "wide")),
        ),
        out_specs=(
            P("narrow", "wide"),
            P("narrow", "wide"),
            P("narrow", "wide"),
            P(),
            P("narrow", "wide"),
            P("narrow", "wide"),
            P("narrow", "wide"),
            P(),
            P(("narrow", "wide")),
            P(("narrow", "wide")),
            P(("narrow", "wide")),
            P(),
        ),
        check_vma=False,
    )
```

profile of v0, /device:TPU:1, one launch (start us, length us, event | category | flops | bytes accessed | tf_op | source)
XLA Modules:
  0.0 378.5 jit_solution(11554978971868273810)
XLA Ops:
  7.2 0.5 broadcast.49
  7.7 1.3 reduce.3
  9.2 1.4 copy.34
  10.6 0.6 copy.31
  11.2 1.6 copy.43
  12.8 1.3 reshape_squeeze.6
  14.1 0.7 copy.42
  15.1 2.5 concatenate.6
  17.8 1.5 reshape.75
  19.4 85.1 %reduce-scatter.4.cloned.1.call-done = f32[1,129,128]{2,1,0:T(8,128)} async-done(((f32[32,129,128]{2,1,0:T(8,128)}), f32[1,129,128]{2,1,0:T(8,128)}) %reduce-scatter.4.cloned.1.call-update) | async-done | bytes 66064
  104.5 1.9 multiply_reduce_fusion.4
  106.3 1.5 multiply_reduce_fusion.2
  107.8 1.0 slice.21
  108.9 0.7 multiply_reduce_fusion
  109.5 78.0 %all-reduce.1 = (f32[]{:T(128)}, f32[]{:T(128)}, f32[]{:T(128)}, f32[]{:T(128)}, f32[]{:T(128)}, /*index=5*/f32[]{:T(128)}) all-reduce(f32[]{:T(128)} %get-tuple-element.13, f32[]{:T(128)} %get-tuple-element.12, f32[]{:T(128)} %get-tuple-element.15, f32[]{:T(128)} %get-tuple-element.14, ...), channel_id=1, replica_groups=mesh['wide'=32,'narrow'=8] {'wide','narrow'}, use_global_device_ids=true, to_apply=%region_2.0 | all-reduce | flops 6 | bytes 48 | tf_op jit(solution)/shard_map/psum | solution.py:89
  191.8 0.6 fusion.4
  192.6 0.5 fusion.3
  193.1 0.6 convert_bitcast_fusion
  193.7 0.7 concatenate.7
  194.5 115.3 %all-gather.2.cloned.1.call-done = bf16[256,129,128]{2,1,0:T(8,128)(2,1)} async-done(((bf16[1,129,128]{2,1,0:T(8,128)(2,1)}), bf16[256,129,128]{2,1,0:T(8,128)(2,1)}) %all-gather.2.cloned.1.call-update) | async-done | bytes 8454160 | tf_op jit(solution)/shard_map/all_gather | solution.py:111
  309.8 13.5 %reshape.81 = bf16[8,32,16512]{2,1,0:T(8,128)(2,1)} reshape(bf16[256,129,128]{2,1,0:T(8,128)(2,1)} %all-gather.2.cloned.1.call-done) | data formatting | bytes 16908288 | tf_op jit(solution)/shard_map/reshape | solution.py:112
  323.4 1.1 slice.33
  324.4 6.0 %slice.32 = bf16[8,32,8192]{2,1,0:T(8,128)(2,1)} slice(bf16[8,32,16512]{2,1,0:T(8,128)(2,1)} %reshape.81), slice={[0:8], [0:32], [8256:16448]} | slice | bytes 8388608 | tf_op jit(solution)/shard_map/slice | solution.py:120
  330.4 2.3 slice.31
  332.8 0.7 reshape.86
  333.5 3.4 copy.36
  336.9 1.0 bitcast_bitcast_fusion
  337.9 2.7 copy.33
  340.6 6.2 %copy.41 = bf16[64,8,32,128]{3,1,2,0:T(8,128)(2,1)} copy(bf16[64,8,32,128]{3,2,1,0:T(8,128)(2,1)S(1)} %bitcast.43) | data formatting | bytes 8388608
  346.8 9.7 %reshape.82 = bf16[8,32,24,344]{3,2,1,0:T(8,128)(2,1)} reshape(bf16[8,32,8256]{2,1,0:T(8,128)(2,1)} %slice.31) | data formatting | bytes 8454144 | tf_op jit(solution)/shard_map/reshape | solution.py:115
  356.5 5.3 %copy.32 = bf16[8,24,32,344]{3,2,1,0:T(8,128)(2,1)} copy(bf16[8,24,32,344]{3,1,2,0:T(8,128)(2,1)} %bitcast.40) | data formatting | bytes 8454144 | tf_op jit(solution)/shard_map/transpose | solution.py:116
  361.8 9.9 %reshape.83 = bf16[192,11008]{1,0:T(8,128)(2,1)} reshape(bf16[8,24,32,344]{3,2,1,0:T(8,128)(2,1)} %copy.32) | data formatting | bytes 8454144 | tf_op jit(solution)/shard_map/reshape | solution.py:117
  (39 shorter events, 0.7 us)
Async XLA Ops:
  7.2 5.6 %copy-start.1 = (f32[1,24,11008]{2,1,0:T(8,128)S(1)}, f32[1,24,11008]{2,1,0:T(8,128)}, u32[]{:S(2)}) copy-start(f32[1,24,11008]{2,1,0:T(8,128)} %param.12) | copy-start | bytes 3170308
  7.2 97.3 %reduce-scatter.4.cloned.1.call-start = ((), (), s32[]{:S(2)}) async-start(), calls=%async_computation.2 | async-start | bytes 2297856
  17.7 86.8 %copy-start.12 = (f32[16]{0:T(128)S(1)}, f32[16]{0:T(128)}, u32[]{:S(2)}) copy-start(f32[16]{0:T(128)} %param.17) | copy-start | bytes 196
  17.7 86.8 %copy-start.13 = (f32[16]{0:T(128)S(1)}, f32[16]{0:T(128)}, u32[]{:S(2)}) copy-start(f32[16]{0:T(128)} %param.20) | copy-start | bytes 196
  17.7 86.8 %copy-start.14 = (f32[16]{0:T(128)S(1)}, f32[16]{0:T(128)}, u32[]{:S(2)}) copy-start(f32[16]{0:T(128)} %param.23) | copy-start | bytes 196
  17.7 88.6 %copy-start.5 = (f32[64,128]{1,0:T(8,128)S(1)}, f32[64,128]{1,0:T(8,128)}, u32[]{:S(2)}) copy-start(f32[64,128]{1,0:T(8,128)} %param.16) | copy-start | bytes 98308
  17.7 88.6 %copy-start.10 = (f32[64,128]{1,0:T(8,128)S(1)}, f32[64,128]{1,0:T(8,128)}, u32[]{:S(2)}) copy-start(f32[64,128]{1,0:T(8,128)} %param.19) | copy-start | bytes 98308
  17.7 88.6 %copy-start.11 = (f32[64,128]{1,0:T(8,128)S(1)}, f32[64,128]{1,0:T(8,128)}, u32[]{:S(2)}) copy-start(f32[64,128]{1,0:T(8,128)} %param.22) | copy-start | bytes 98308
  17.7 91.1 %copy-start.2 = (f32[24,344]{1,0:T(8,128)S(1)}, f32[24,344]{1,0:T(8,128)}, u32[]{:S(2)}) copy-start(f32[24,344]{1,0:T(8,128)} %param.15) | copy-start | bytes 99076
  17.8 91.1 %copy-start.8 = (f32[24,344]{1,0:T(8,128)S(1)}, f32[24,344]{1,0:T(8,128)}, u32[]{:S(2)}) copy-start(f32[24,344]{1,0:T(8,128)} %param.21) | copy-start | bytes 99076
  17.8 91.1 %copy-start.9 = (f32[24,344]{1,0:T(8,128)S(1)}, f32[24,344]{1,0:T(8,128)}, u32[]{:S(2)}) copy-start(f32[24,344]{1,0:T(8,128)} %param.18) | copy-start | bytes 99076
  19.3 290.4 %all-gather.2.cloned.1.call-start = ((), (), s32[]{:S(2)}) async-start(), calls=%async_computation.1 | async-start | bytes 8947712 | tf_op jit(solution)/shard_map/all_gather | solution.py:111
  107.8 215.5 %copy-start.6 = (f32[64,128]{1,0:T(8,128)}, f32[64,128]{1,0:T(8,128)S(1)}, u32[]{:S(2)}) copy-start(f32[64,128]{1,0:T(8,128)S(1)} %get-tuple-element.32) | copy-start | bytes 98308
  107.8 215.5 %copy-start.7 = (f32[64,128]{1,0:T(8,128)}, f32[64,128]{1,0:T(8,128)S(1)}, u32[]{:S(2)}) copy-start(f32[64,128]{1,0:T(8,128)S(1)} %get-tuple-element.33) | copy-start | bytes 98308
  109.5 213.8 %copy-start.3 = (f32[24,344]{1,0:T(8,128)}, f32[24,344]{1,0:T(8,128)S(1)}, u32[]{:S(2)}) copy-start(f32[24,344]{1,0:T(8,128)S(1)} %get-tuple-element.34) | copy-start | bytes 99076
  109.5 213.8 %copy-start.4 = (f32[24,344]{1,0:T(8,128)}, f32[24,344]{1,0:T(8,128)S(1)}, u32[]{:S(2)}) copy-start(f32[24,344]{1,0:T(8,128)S(1)} %get-tuple-element.35) | copy-start | bytes 99076
  323.4 7.1 %copy-start = (bf16[8,32,16512]{2,1,0:T(8,128)(2,1)S(1)}, bf16[8,32,16512]{2,1,0:T(8,128)(2,1)}, u32[]{:S(2)}) copy-start(bf16[8,32,16512]{2,1,0:T(8,128)(2,1)} %reshape.81) | copy-start | bytes 25362436
Sparse Core Ops, SparseCore 0:
  19.5 84.9 reduce-scatter.3
  194.6 115.1 all-gather.1
where the time goes:
time: 380 us; the launch traced here: 378 us
  waiting for transfers between devices  200 us (53%)
  blocking collectives  78 us (21%)
  local copies, waits for them, and re-layouts  74.3 us (20%)
  between operations  18.5 us (5%)
  other arithmetic  7.16 us (2%)
    all_gather x1, waiting for transfers between devices, body(): whole = lax.all_gather(low, ('narrow', 'wide'), axis=0, tiled=True)  115 us
    unnamed x3, waiting for transfers between devices  85.1 us
    psum x1, blocking collectives, body(): lax.psum((weight_sums, (jnp.sum(up_update * up_update), jnp.sum(down_upda...  78 us
    reshape x2, local copies, waits for them, and re-layouts, body(): up_weights = whole[:, :, :up_size].reshape(n_narrow, n_wide, up_rows, up_...  19.5 us
    reshape x1, local copies, waits for them, and re-layouts, body(): whole = whole.reshape(n_narrow, n_wide, width)  13.5 us
    unnamed x35, local copies, waits for them, and re-layouts  13.1 us
  transfers between devices with their start and end apart: 2, of which 2 were waited for; matrix products, arithmetic and copies ran while one was open for 0% of the time, Pallas kernels for 0%

commit v1 on v0

--- a/solution.py
+++ b/solution.py
@@ -108,7 +108,15 @@
             jnp.zeros((width - total,), jnp.bfloat16),
         ]
     ).reshape(1, width // LANES, LANES)
-    whole = lax.all_gather(low, ("narrow", "wide"), axis=0, tiled=True)
+    whole = jnp.concatenate(
+        lax.all_to_all(
+            jnp.stack([low for _ in range(lax.axis_size(("narrow", "wide")))]),
+            ("narrow", "wide"),
+            0,
+            0,
+        ),
+        axis=0,
+    )
     whole = whole.reshape(n_narrow, n_wide, width)
     up_weights = (
         whole[:, :, :up_size]

time: 380 us -> 472 us (1.24)
  blocking collectives: 78 us -> 285 us
  waiting for transfers between devices: 200 us -> 85.1 us
    all_to_all x0 -> x1, blocking collectives: none -> 207 us  [body(): lax.all_to_all(jnp.stack([low for _ in range(lax.axis_size(('narrow', 'wi...]
    all_gather x1 -> x0, waiting for transfers between devices: 115 us -> none  [body(): whole = lax.all_gather(low, ('narrow', 'wide'), axis=0, tiled=True)]
    another operation x0 -> x2, local copies, waits for them, and re-layouts: none -> 14.7 us  [the longest x1 13.5 us: body(): whole = whole.reshape(n_narrow, n_wide, width)]
    reshape x1 -> x0, local copies, waits for them, and re-layouts: 13.5 us -> none  [body(): whole = whole.reshape(n_narrow, n_wide, width)]
    unnamed x3 -> x2, waiting for transfers between devices: 85.1 us -> 85.1 us
  transfers between devices with their start and end apart: 2 -> 1, of which waited for: 2 -> 1; matrix products, arithmetic and copies ran while one was open for 0% -> 0% of each run, Pallas kernels for 0% -> 0%
where the time goes in v1:
time: 472 us; the launch traced here: 471 us
  blocking collectives  285 us (60%)
  waiting for transfers between devices  85.1 us (18%)
  local copies, waits for them, and re-layouts  74.8 us (16%)
  between operations  18.5 us (4%)
  other arithmetic  7.15 us (2%)
    all_to_all x1, blocking collectives, body(): lax.all_to_all(jnp.stack([low for _ in range(lax.axis_size(('narrow', 'wi...  207 us
    unnamed x2, waiting for transfers between devices  85.1 us
    psum x1, blocking collectives, body(): lax.psum((weight_sums, (jnp.sum(up_update * up_update), jnp.sum(down_upda...  78 us
    reshape x2, local copies, waits for them, and re-layouts, body(): up_weights = whole[:, :, :up_size].reshape(n_narrow, n_wide, up_rows, up_...  19.5 us
    another operation x1, local copies, waits for them, and re-layouts, body(): whole = whole.reshape(n_narrow, n_wide, width)  13.5 us
    unnamed x35, local copies, waits for them, and re-layouts  13.1 us
  transfers between devices with their start and end apart: 1, of which 1 were waited for; matrix products, arithmetic and copies ran while one was open for 0% of the time, Pallas kernels for 0%

profile of v1, /device:TPU:1, one launch (start us, length us, event | category | flops | bytes accessed | tf_op | source)
XLA Modules:
  0.0 470.9 jit_solution(5889122398310783000)
XLA Ops:
  7.2 0.5 broadcast.51
  7.7 1.3 reduce.3
  9.2 1.4 copy.34
  10.6 0.6 copy.31
  11.2 1.6 copy.43
  12.8 1.3 reshape_squeeze.6
  14.1 0.7 copy.42
  15.1 2.5 concatenate.6
  17.8 1.5 reshape.73
  19.3 85.1 %reduce-scatter.4.cloned.1.call-done = f32[1,129,128]{2,1,0:T(8,128)} async-done(((f32[32,129,128]{2,1,0:T(8,128)}), f32[1,129,128]{2,1,0:T(8,128)}) %reduce-scatter.4.cloned.1.call-update) | async-done | bytes 66064
  104.5 1.9 multiply_reduce_fusion.4
  106.3 1.5 multiply_reduce_fusion.2
  107.8 1.0 slice.21
  108.9 0.7 multiply_reduce_fusion
  109.5 78.0 %all-reduce.1 = (f32[]{:T(128)}, f32[]{:T(128)}, f32[]{:T(128)}, f32[]{:T(128)}, f32[]{:T(128)}, /*index=5*/f32[]{:T(128)}) all-reduce(f32[]{:T(128)} %get-tuple-element.13, f32[]{:T(128)} %get-tuple-element.12, f32[]{:T(128)} %get-tuple-element.15, f32[]{:T(128)} %get-tuple-element.14, ...), channel_id=1, replica_groups=mesh['wide'=32,'narrow'=8] {'wide','narrow'}, use_global_device_ids=true, to_apply=%region_2.0 | all-reduce | flops 6 | bytes 48 | tf_op jit(solution)/shard_map/psum | solution.py:89
  191.8 0.6 fusion.4
  192.6 0.5 fusion.3
  193.1 0.6 convert_bitcast_fusion
  193.9 1.1 stack.3
  195.0 207.3 %all_to_all.5 = bf16[256,1,129,128]{3,2,1,0:T(8,128)(2,1)} all-to-all(bf16[256,1,129,128]{3,2,1,0:T(8,128)(2,1)S(1)} %stack.3), channel_id=1, replica_groups=mesh['wide'=32,'narrow'=8] {'narrow','wide'}, dimensions={0} | all-to-all | bytes 16908288 | tf_op jit(solution)/shard_map/all_to_all | solution.py:112
  402.3 13.5 %reshape_reshape.3 = bf16[8,32,16512]{2,1,0:T(8,128)(2,1)} reshape(bf16[256,1,129,128]{3,2,1,0:T(8,128)(2,1)} %all_to_all.5) | data formatting | bytes 16908288 | tf_op jit(solution)/shard_map/reshape;reshape | solution.py:120
  415.8 1.1 slice.33
  416.9 6.0 %slice.32 = bf16[8,32,8192]{2,1,0:T(8,128)(2,1)} slice(bf16[8,32,16512]{2,1,0:T(8,128)(2,1)} %reshape_reshape.3), slice={[0:8], [0:32], [8256:16448]} | slice | bytes 8388608 | tf_op jit(solution)/shard_map/slice | solution.py:128
  422.9 2.3 slice.31
  425.2 0.7 reshape.82
  425.9 3.4 copy.36
  429.3 1.0 bitcast_bitcast_fusion
  430.4 2.7 copy.33
  433.1 6.2 %copy.41 = bf16[64,8,32,128]{3,1,2,0:T(8,128)(2,1)} copy(bf16[64,8,32,128]{3,2,1,0:T(8,128)(2,1)S(1)} %bitcast.43) | data formatting | bytes 8388608
  439.2 9.7 %reshape.78 = bf16[8,32,24,344]{3,2,1,0:T(8,128)(2,1)} reshape(bf16[8,32,8256]{2,1,0:T(8,128)(2,1)} %slice.31) | data formatting | bytes 8454144 | tf_op jit(solution)/shard_map/reshape | solution.py:123
  448.9 5.3 %copy.32 = bf16[8,24,32,344]{3,2,1,0:T(8,128)(2,1)} copy(bf16[8,24,32,344]{3,1,2,0:T(8,128)(2,1)} %bitcast.40) | data formatting | bytes 8454144 | tf_op jit(solution)/shard_map/transpose | solution.py:124
  454.2 9.9 %reshape.79 = bf16[192,11008]{1,0:T(8,128)(2,1)} reshape(bf16[8,24,32,344]{3,2,1,0:T(8,128)(2,1)} %copy.32) | data formatting | bytes 8454144 | tf_op jit(solution)/shard_map/reshape | solution.py:125
  (38 shorter events, 0.8 us)
Async XLA Ops:
  7.2 5.6 %copy-start.1 = (f32[1,24,11008]{2,1,0:T(8,128)S(1)}, f32[1,24,11008]{2,1,0:T(8,128)}, u32[]{:S(2)}) copy-start(f32[1,24,11008]{2,1,0:T(8,128)} %param.12) | copy-start | bytes 3170308
  7.2 97.3 %reduce-scatter.4.cloned.1.call-start = ((), (), s32[]{:S(2)}) async-start(), calls=%async_computation.2 | async-start | bytes 2297856
  17.7 86.8 %copy-start.12 = (f32[16]{0:T(128)S(1)}, f32[16]{0:T(128)}, u32[]{:S(2)}) copy-start(f32[16]{0:T(128)} %param.17) | copy-start | bytes 196
  17.7 86.8 %copy-start.13 = (f32[16]{0:T(128)S(1)}, f32[16]{0:T(128)}, u32[]{:S(2)}) copy-start(f32[16]{0:T(128)} %param.20) | copy-start | bytes 196
  17.7 86.8 %copy-start.14 = (f32[16]{0:T(128)S(1)}, f32[16]{0:T(128)}, u32[]{:S(2)}) copy-start(f32[16]{0:T(128)} %param.23) | copy-start | bytes 196
  17.7 88.6 %copy-start.5 = (f32[64,128]{1,0:T(8,128)S(1)}, f32[64,128]{1,0:T(8,128)}, u32[]{:S(2)}) copy-start(f32[64,128]{1,0:T(8,128)} %param.16) | copy-start | bytes 98308
  17.7 88.6 %copy-start.10 = (f32[64,128]{1,0:T(8,128)S(1)}, f32[64,128]{1,0:T(8,128)}, u32[]{:S(2)}) copy-start(f32[64,128]{1,0:T(8,128)} %param.19) | copy-start | bytes 98308
  17.7 88.6 %copy-start.11 = (f32[64,128]{1,0:T(8,128)S(1)}, f32[64,128]{1,0:T(8,128)}, u32[]{:S(2)}) copy-start(f32[64,128]{1,0:T(8,128)} %param.22) | copy-start | bytes 98308
  17.7 91.1 %copy-start.2 = (f32[24,344]{1,0:T(8,128)S(1)}, f32[24,344]{1,0:T(8,128)}, u32[]{:S(2)}) copy-start(f32[24,344]{1,0:T(8,128)} %param.15) | copy-start | bytes 99076
  17.8 91.1 %copy-start.8 = (f32[24,344]{1,0:T(8,128)S(1)}, f32[24,344]{1,0:T(8,128)}, u32[]{:S(2)}) copy-start(f32[24,344]{1,0:T(8,128)} %param.21) | copy-start | bytes 99076
  17.8 91.1 %copy-start.9 = (f32[24,344]{1,0:T(8,128)S(1)}, f32[24,344]{1,0:T(8,128)}, u32[]{:S(2)}) copy-start(f32[24,344]{1,0:T(8,128)} %param.18) | copy-start | bytes 99076
  107.8 87.2 %copy-start.6 = (f32[64,128]{1,0:T(8,128)}, f32[64,128]{1,0:T(8,128)S(1)}, u32[]{:S(2)}) copy-start(f32[64,128]{1,0:T(8,128)S(1)} %get-tuple-element.32) | copy-start | bytes 98308
  107.8 87.2 %copy-start.7 = (f32[64,128]{1,0:T(8,128)}, f32[64,128]{1,0:T(8,128)S(1)}, u32[]{:S(2)}) copy-start(f32[64,128]{1,0:T(8,128)S(1)} %get-tuple-element.33) | copy-start | bytes 98308
  109.5 85.5 %copy-start.3 = (f32[24,344]{1,0:T(8,128)}, f32[24,344]{1,0:T(8,128)S(1)}, u32[]{:S(2)}) copy-start(f32[24,344]{1,0:T(8,128)S(1)} %get-tuple-element.34) | copy-start | bytes 99076
  109.5 85.5 %copy-start.4 = (f32[24,344]{1,0:T(8,128)}, f32[24,344]{1,0:T(8,128)S(1)}, u32[]{:S(2)}) copy-start(f32[24,344]{1,0:T(8,128)S(1)} %get-tuple-element.35) | copy-start | bytes 99076
  415.8 7.1 %copy-start = (bf16[8,32,16512]{2,1,0:T(8,128)(2,1)S(1)}, bf16[8,32,16512]{2,1,0:T(8,128)(2,1)}, u32[]{:S(2)}) copy-start(bf16[8,32,16512]{2,1,0:T(8,128)(2,1)} %reshape_reshape.3) | copy-start | bytes 25362436
Sparse Core Ops, SparseCore 0:
  19.5 84.9 reduce-scatter.3
